TPU v7x, 128 devices: a whole 4x4x4 slice. The times are simulated.
128 devices in a mesh: seq: 16 (over x_hi, z, core), tp: 8 (over y, x_lo).
Axes of the slice: x: 4 (x_hi: 2, x_lo: 2; x = x_hi * 2 + x_lo), y: 4, z: 4, core: 2. Of those that a mesh axis runs over, the one named last changes fastest.
Arguments:
- tokens: bfloat16 [4, 2048, 4096], P(None, 'seq', 'tp'), may hold values from -6 to 6
- new_tokens: bfloat16 [4, 4096], P(None, 'tp'), may hold values from -6 to 6
- w_qkv: bfloat16 [3, 4096, 4096], P(None, None, 'tp')
- w_out: bfloat16 [4096, 4096], P('tp')
- q_gain: float32 [4096], P('tp'), may hold values from 0.5 to 6
- k_gain: float32 [4096], P('tp'), may hold values from 0.5 to 6
- post_gain: float32 [4096], P('tp'), may hold values from 0.5 to 1.5
- lengths: int32 [4], replicated, may hold values from 1 to 2048, 6144 in all
Outputs:
- hidden_out: bfloat16 [4, 2048, 4096], P(None, 'seq', 'tp')
- new_out: bfloat16 [4, 4096], P(None, 'tp')
Inputs may be any that keep to these rules, and one draw needn't show every extreme that they name: `lengths`: one prompt has exactly 2048 live tokens.
All inputs are finite; a program needn't handle non-finite values.
Results may differ from a plain program's by a relative error of at most 0.012.
The roundings to bfloat16 on the way count: a program that leaves them out, or rounds other values in their place, can miss the bound.
Values may be sent and summed in bfloat16 or wider, within the bound.
No kernel may reach another device: no remote copies, remote signals or barrier semaphores. Data moves between devices by JAX's collectives and lax.ppermute only.
A program may use at most 128 MiB of HBM per device.

v0:
```python
import jax
import jax.numpy as jnp
from jax import lax
from jax.sharding import PartitionSpec as P

HD = 128
rope_base = 500000.0
norm_eps = 1e-06
masked_fill = -1e30


def rotate(values, position):
    half = values.shape[-1] // 2
    freq = rope_base ** (-(jnp.arange(half, dtype=jnp.float32) * 2.0) / values.shape[-1])
    angle = position.astype(jnp.float32)[..., None] * freq
    cosine = jnp.cos(angle)
    sine = jnp.sin(angle)
    lower = values[..., :half]
    upper = values[..., half:]
    return jnp.concatenate([lower * cosine - upper * sine, upper * cosine + lower * sine], -1)


def attend_pair(q_all, k_all, v_all, q_new, k_new, v_new, length):
    count = q_all.shape[0]
    scale = HD ** (-0.5)
    scores = jnp.dot(q_all, k_all.T, preferred_element_type=jnp.float32) * scale
    query_pos = jnp.arange(count, dtype=jnp.int32)[:, None]
    key_pos = jnp.arange(count, dtype=jnp.int32)[None, :]
    valid = (key_pos <= query_pos) & (key_pos < length)
    scores = jnp.where(valid, scores, masked_fill)
    top = jnp.max(scores, -1, keepdims=True)
    weights = jnp.where(valid, jnp.exp(scores - top), 0.0)
    total = jnp.sum(weights, -1, keepdims=True)
    prompt_out = (
        jnp.dot(weights.astype(jnp.bfloat16), v_all, preferred_element_type=jnp.float32) / total
    ).astype(jnp.bfloat16)
    new_scores = jnp.dot(k_all, q_new, preferred_element_type=jnp.float32) * scale
    live = jnp.arange(count, dtype=jnp.int32) < length
    new_scores = jnp.where(live, new_scores, masked_fill)
    self_score = jnp.dot(q_new, k_new, preferred_element_type=jnp.float32) * scale
    new_top = jnp.maximum(jnp.max(new_scores), self_score)
    new_weights = jnp.where(live, jnp.exp(new_scores - new_top), 0.0)
    own_weight = jnp.exp(self_score - new_top)
    new_total = jnp.sum(new_weights) + own_weight
    own_rounded = lax.optimization_barrier(own_weight.astype(jnp.bfloat16)).astype(jnp.float32)
    numer = jnp.dot(new_weights.astype(jnp.bfloat16), v_all, preferred_element_type=jnp.float32)
    numer = numer + own_rounded * v_new.astype(jnp.float32)
    return (prompt_out, (numer / new_total).astype(jnp.bfloat16))


def body(tokens, new_tokens, w_qkv, w_out, q_gain, k_gain, post_gain, lengths):
    seqs, pos_dev, width_local = tokens.shape
    heads_local = width_local // HD
    full_width = w_qkv.shape[1]
    n_seq = lax.axis_size("seq")
    pairs = seqs * heads_local
    assert pairs == n_seq
    prompt_rows = seqs * pos_dev
    full_len = pos_dev * n_seq
    flat_rows = tokens.reshape(prompt_rows, width_local)
    local_rows = jnp.concatenate([flat_rows, new_tokens], 0)
    all_rows = lax.all_gather(local_rows, "tp", axis=1, tiled=True)
    proj = jnp.einsum("tn,cnf->ctf", all_rows, w_qkv, preferred_element_type=jnp.float32)
    query_raw, key_raw = (proj[0], proj[1])
    query_sq, key_sq = lax.psum(
        (jnp.sum(query_raw * query_raw, -1), jnp.sum(key_raw * key_raw, -1)), "tp"
    )

    def normed(values, square_sum, gain):
        return values * lax.rsqrt(square_sum[:, None] / full_width + norm_eps) * gain

    seq_index = lax.axis_index("seq")
    query_pos = seq_index * pos_dev + jnp.arange(pos_dev, dtype=jnp.int32)
    row_pos = jnp.concatenate([jnp.tile(query_pos, seqs), lengths.astype(jnp.int32)], 0)
    rows_all = prompt_rows + seqs
    queries = rotate(
        normed(query_raw, query_sq, q_gain).reshape(rows_all, heads_local, HD), row_pos[:, None]
    ).astype(jnp.bfloat16)
    keys = rotate(
        normed(key_raw, key_sq, k_gain).reshape(rows_all, heads_local, HD), row_pos[:, None]
    ).astype(jnp.bfloat16)
    values = proj[2].astype(jnp.bfloat16).reshape(rows_all, heads_local, HD)
    qkv = jnp.stack([queries[:prompt_rows], keys[:prompt_rows], values[:prompt_rows]], 0)
    qkv = qkv.reshape(3, seqs, pos_dev, heads_local, HD).transpose(1, 3, 0, 2, 4)
    qkv = qkv.reshape(pairs, 3, pos_dev, HD)
    got = lax.all_to_all(qkv, "seq", 0, 0, tiled=True)
    full = got.transpose(1, 0, 2, 3).reshape(3, full_len, HD)
    owner = seq_index
    own_prompt = owner // heads_local
    new_q = queries[prompt_rows:].reshape(pairs, HD)[owner]
    new_k = keys[prompt_rows:].reshape(pairs, HD)[owner]
    new_v = values[prompt_rows:].reshape(pairs, HD)[owner]
    prompt_out, new_out = attend_pair(
        full[0], full[1], full[2], new_q, new_k, new_v, lengths[own_prompt]
    )
    pad = 8
    back = jnp.concatenate(
        [prompt_out.reshape(n_seq, pos_dev, HD), jnp.broadcast_to(new_out, (n_seq, pad, HD))], 1
    )
    ret = lax.all_to_all(back, "seq", 0, 0, tiled=True)
    ret = ret.reshape(seqs, heads_local, pos_dev + pad, HD)
    attn_rows = ret[:, :, :pos_dev].transpose(0, 2, 1, 3).reshape(prompt_rows, width_local)
    attn_new = ret[:, :, pos_dev].reshape(seqs, width_local)
    attention = jnp.concatenate([attn_rows, attn_new], 0)
    part = jnp.dot(attention, w_out, preferred_element_type=jnp.float32)
    summed = lax.psum_scatter(
        part.astype(jnp.bfloat16), "tp", scatter_dimension=1, tiled=True
    ).astype(jnp.float32)
    square = lax.psum(jnp.sum(summed * summed, -1), "tp")
    out = (
        local_rows.astype(jnp.float32)
        + summed * lax.rsqrt(square[:, None] / full_width + norm_eps) * post_gain
    ).astype(jnp.bfloat16)
    return (out[:prompt_rows].reshape(seqs, pos_dev, width_local), out[prompt_rows:])


def solution(mesh):
    in_specs = (
        P(None, "seq", "tp"),
        P(None, "tp"),
        P(None, None, "tp"),
        P("tp", None),
        P("tp"),
        P("tp"),
        P("tp"),
        P(),
    )
    out_specs = (P(None, "seq", "tp"), P(None, "tp"))
    return jax.shard_map(body, mesh=mesh, in_specs=in_specs, out_specs=out_specs, check_vma=False)
```

profile of v0, /device:TPU:4, one launch (start us, length us, event | category | flops | bytes accessed | tf_op | source)
XLA Modules:
  0.0 334.7 jit_solution(7153203666881482094)
XLA Ops:
  7.2 0.0 copy-start.9
  7.2 0.0 all-gather.2.cloned.1.call-start
  7.2 1.9 pad_maximum_fusion.2
  9.1 0.0 all-gather.2.cloned.1.call-update
  9.2 0.0 copy-done.9
  9.2 1.7 multiply_cosine_fusion
  11.0 92.7 %all-gather.2.cloned.1.call-done = bf16[516,4096]{1,0:T(8,128)(2,1)} async-done(((bf16[516,512]{1,0:T(8,128)(2,1)}), bf16[516,4096]{1,0:T(8,128)(2,1)}) %all-gather.2.cloned.1.call-update) | async-done | bytes 4227088 | tf_op jit(solution)/shard_map/all_gather | solution.py:62
  103.7 10.6 %fusion.45 = (bf16[3,516,512]{2,1,0:T(8,128)(2,1)S(1)}, f32[3,516,512]{2,1,0:T(8,128)S(1)}) fusion(bf16[3,4096,512]{2,1,0:T(8,128)(2,1)} %param.10, bf16[516,4096]{1,0:T(8,128)(2,1)} %all-gather.2.cloned.1.call-done), kind=kOutput, calls=%fused_computation.82 | convolution fusion | flops 6493575168 | bytes 21565440 | tf_op jit(solution)/shard_map/tn,cnf->ctf/dot_general | solution.py:63
  114.3 0.0 copy-start.4
  114.3 0.3 multiply_reduce_fusion.1
  114.7 0.8 copy-done.4
  115.5 0.1 stack.14
  115.7 0.9 copy.12
  116.6 0.4 squeeze.27
  116.9 0.0 copy-start.6
  116.9 0.4 squeeze.28
  117.3 0.0 copy-start.7
  117.3 18.3 %all-reduce = (f32[516]{0:T(1024)S(1)}, f32[516]{0:T(1024)S(1)}) all-reduce(f32[516]{0:T(1024)S(1)} %get-tuple-element.3, f32[516]{0:T(1024)S(1)} %get-tuple-element.2), channel_id=1, replica_groups=mesh['seq'=16,'tp'=8] {'tp'}, use_global_device_ids=true, to_apply=%region_3.0 | all-reduce | flops 1032 | bytes 8256 | tf_op jit(solution)/shard_map/psum | solution.py:65
  135.7 0.0 copy-done.6
  135.7 1.5 multiply_multiply_fusion.1
  137.2 0.0 copy-start.3
  137.2 0.0 copy-done.7
  137.2 1.5 multiply_multiply_fusion
  138.8 0.0 copy-done.3
  138.8 1.7 add_convert_fusion.1
  140.5 0.7 fusion.27
  141.3 0.1 copy.10
  141.4 0.0 copy-start.2
  141.4 0.7 fusion.26
  142.1 0.1 copy.11
  142.2 0.2 copy-done.2
  142.4 1.3 pad_maximum_fusion
  143.7 7.4 %all-to-all-start = ((bf16[16,3,128,128]{3,2,1,0:T(8,128)(2,1)}), bf16[16,3,128,128]{3,2,1,0:T(8,128)(2,1)S(1)}, u32[]{:S(2)}, u32[]{:S(2)}) async-start(bf16[16,3,128,128]{3,2,1,0:T(8,128)(2,1)} %bitcast.10), calls=%async_computation | async-start | bytes 3145728 | tf_op jit(solution)/shard_map/all_to_all | solution.py:86
  151.1 0.2 reduce-scatter.2.cloned.1.call-start
  151.4 0.6 dynamic_slice.12
  152.0 0.7 iota_compare_fusion.1
  152.6 0.7 slice.101
  153.3 0.8 pad_maximum_fusion.4
  154.1 0.1 pad_maximum_fusion.3
  154.2 0.6 fusion.34
  155.4 16.7 %all-to-all-done = bf16[16,3,128,128]{3,2,1,0:T(8,128)(2,1)S(1)} async-done(((bf16[16,3,128,128]{3,2,1,0:T(8,128)(2,1)}), bf16[16,3,128,128]{3,2,1,0:T(8,128)(2,1)S(1)}, u32[]{:S(2)}, u32[]{:S(2)}) %all-to-all-start) | async-done | bytes 1572896 | tf_op jit(solution)/shard_map/all_to_all | solution.py:86
  172.1 0.1 fusion.44
  172.2 0.2 fusion.38
  172.4 1.3 fusion.28
  174.4 1.3 fusion.29
  176.3 5.9 %fusion.1 = (f32[2048]{0:T(1024)S(1)}, f32[2048,2048]{0,1:T(8,128)S(1)}) fusion(pred[2048]{0:T(1024)(128)(4,1)S(1)} %iota_compare_fusion.1, bf16[2048,128]{1,0:T(8,128)(2,1)S(1)} %bitcast.92, bf16[2048,128]{1,0:T(8,128)(2,1)S(1)} %bitcast.88), kind=kOutput, calls=%fused_computation.4 | convolution fusion | flops 1094711296 | bytes 17836032 | tf_op jit(solution)/shard_map/dot_general | solution.py:26
  182.2 8.4 %fusion.6 = f32[2048]{0:T(1024)S(1)} fusion(f32[2048]{0:T(1024)S(1)} %get-tuple-element.23, f32[2048,2048]{0,1:T(8,128)S(1)} %get-tuple-element.24, pred[2048]{0:T(1024)(128)(4,1)S(1)} %iota_compare_fusion.1), kind=kLoop, calls=%fused_computation.10 | loop fusion | flops 29358080 | bytes 16795648 | tf_op jit(solution)/shard_map/reduce_sum | solution.py:33
  190.6 3.5 %fusion.10 = bf16[2048,128]{1,0:T(8,128)(2,1)S(1)} fusion(bf16[2048,128]{1,0:T(8,128)(2,1)S(1)} %bitcast.85, f32[2048]{0:T(1024)S(1)} %get-tuple-element.23, f32[2048,2048]{0,1:T(8,128)S(1)} %get-tuple-element.24, pred[2048]{0:T(1024)(128)(4,1)S(1)} %iota_compare_fusion.1, f32[2048]{0:T(1024)S(1)} %fusion.6), kind=kOutput, calls=%fused_computation.12 | convolution fusion | flops 1103626240 | bytes 17844224 | tf_op jit(solution)/shard_map/dot_general | solution.py:35
  194.1 0.2 fusion.18
  194.4 0.0 copy-start.10
  194.4 17.3 %all_to_all.10 = bf16[16,136,128]{2,1,0:T(8,128)(2,1)S(1)} all-to-all(bf16[16,136,128]{2,1,0:T(8,128)(2,1)S(1)} %pad_maximum_fusion.1), channel_id=1, replica_groups=mesh['seq'=16,'tp'=8] {'seq'}, dimensions={0} | all-to-all | bytes 1114112 | tf_op jit(solution)/shard_map/all_to_all | solution.py:100
  211.7 0.1 copy.13
  211.8 0.2 slice_bitcast_fusion
  212.0 0.2 copy.14
  212.2 0.1 copy.22
  212.3 0.0 copy-done.10
  212.3 4.4 %convolution_convert_fusion = bf16[516,4096]{1,0:T(8,128)(2,1)} fusion(bf16[512,4096]{1,0:T(8,128)(2,1)S(1)} %copy-done.10, bf16[4,512]{1,0:T(4,128)(2,1)S(1)} %bitcast.98, bf16[512,512]{1,0:T(8,128)(2,1)S(1)} %bitcast.91), kind=kOutput, calls=%fused_computation.7 | convolution fusion | flops 2167431168 | bytes 8949760 | tf_op jit(solution)/shard_map/dot_general | solution.py:105
  216.6 0.0 reduce-scatter.2.cloned.1.call-update
  216.7 89.1 %reduce-scatter.2.cloned.1.call-done = bf16[516,512]{1,0:T(8,128)(2,1)} async-done(((bf16[516,4096]{1,0:T(8,128)(2,1)}), bf16[516,512]{1,0:T(8,128)(2,1)}) %reduce-scatter.2.cloned.1.call-update) | async-done | bytes 528400 | tf_op jit(solution)/shard_map/reduce_scatter | solution.py:106
  305.8 1.2 fusion.19
  307.0 18.0 %psum.23 = f32[516]{0:T(1024)S(1)} all-reduce(f32[516]{0:T(1024)S(1)} %fusion.19), channel_id=1, replica_groups=mesh['seq'=16,'tp'=8] {'tp'}, use_global_device_ids=true, to_apply=%region_10.11 | all-reduce | flops 516 | bytes 4128 | tf_op jit(solution)/shard_map/psum | solution.py:109
  325.1 1.3 fusion.22
  326.4 0.6 slice.105
  327.0 0.8 slice.104
  (21 shorter events, 0.2 us)
Async XLA Ops:
  7.2 2.0 copy-start.9
  7.2 96.5 %all-gather.2.cloned.1.call-start = ((), (), s32[]{:S(2)}) async-start(), calls=%async_computation.3 | async-start | bytes 4792320 | tf_op jit(solution)/shard_map/all_gather | solution.py:62
  114.3 1.2 copy-start.4
  116.9 18.8 %copy-start.6 = (f32[512]{0:T(512)S(1)}, f32[512]{0:T(512)}, u32[]{:S(2)}) copy-start(f32[512]{0:T(512)} %param.12) | copy-start | bytes 6148
  117.3 19.9 %copy-start.7 = (f32[512]{0:T(512)S(1)}, f32[512]{0:T(512)}, u32[]{:S(2)}) copy-start(f32[512]{0:T(512)} %param.13) | copy-start | bytes 6148
  137.2 1.6 copy-start.3
  140.5 1.6 copy-start
  141.4 1.0 copy-start.2
  143.7 28.4 %all-to-all-start = ((bf16[16,3,128,128]{3,2,1,0:T(8,128)(2,1)}), bf16[16,3,128,128]{3,2,1,0:T(8,128)(2,1)S(1)}, u32[]{:S(2)}, u32[]{:S(2)}) async-start(bf16[16,3,128,128]{3,2,1,0:T(8,128)(2,1)} %bitcast.10), calls=%async_computation | async-start | bytes 3145728 | tf_op jit(solution)/shard_map/all_to_all | solution.py:86
  151.1 154.7 %reduce-scatter.2.cloned.1.call-start = ((), (), s32[]{:S(2)}) async-start(), calls=%async_computation.4 | async-start | bytes 4792320 | tf_op jit(solution)/shard_map/reduce_scatter | solution.py:106
  194.4 17.9 %copy-start.10 = (bf16[512,4096]{1,0:T(8,128)(2,1)S(1)}, bf16[512,4096]{1,0:T(8,128)(2,1)}, u32[]{:S(2)}) copy-start(bf16[512,4096]{1,0:T(8,128)(2,1)} %param.11) | copy-start | bytes 12582916
  216.6 108.4 %copy-start.1 = (bf16[4,128,512]{2,1,0:T(8,128)(2,1)S(1)}, bf16[4,128,512]{2,1,0:T(8,128)(2,1)}, u32[]{:S(2)}) copy-start(bf16[4,128,512]{2,1,0:T(8,128)(2,1)} %param.8) | copy-start | bytes 1572868
  216.6 108.4 %copy-start.5 = (bf16[4,512]{1,0:T(4,128)(2,1)S(1)}, bf16[4,512]{1,0:T(4,128)(2,1)}, u32[]{:S(2)}) copy-start(bf16[4,512]{1,0:T(4,128)(2,1)} %param.9) | copy-start | bytes 12292
  216.6 108.4 %copy-start.8 = (f32[512]{0:T(512)S(1)}, f32[512]{0:T(512)}, u32[]{:S(2)}) copy-start(f32[512]{0:T(512)} %param.14) | copy-start | bytes 6148
Sparse Core Ops, SparseCore 0:
  9.7 93.9 all-gather.1
  216.8 88.9 reduce-scatter.1
where the time goes:
time: 335 us
  waiting for transfers between devices  199 us (59%)
  blocking collectives  53.6 us (16%)
  other arithmetic  27.2 us (8%)
  matrix products  24.8 us (7%)
  between operations  16.4 us (5%)
  starting transfers between devices  7.66 us (2%)
  local copies, waits for them, and re-layouts  6.41 us (2%)
    all_gather x1, waiting for transfers between devices, body(): all_rows = lax.all_gather(local_rows, 'tp', axis=1, tiled=True)  92.7 us
    reduce_scatter x1, waiting for transfers between devices, body(): lax.psum_scatter(part.astype(jnp.bfloat16), 'tp', scatter_dimension=1, ti...  89.1 us
    psum x1, blocking collectives, body(): lax.psum((jnp.sum(query_raw * query_raw, -1), jnp.sum(key_raw * key_raw,...  18.3 us
    psum x1, blocking collectives, body(): square = lax.psum(jnp.sum(summed * summed, -1), 'tp')  18 us
    all_to_all x1, blocking collectives, body(): ret = lax.all_to_all(back, 'seq', 0, 0, tiled=True)  17.3 us
    all_to_all x1, waiting for transfers between devices, body(): got = lax.all_to_all(qkv, 'seq', 0, 0, tiled=True)  16.7 us
    dot_general x1, matrix products, body(): jnp.einsum('tn,cnf->ctf', all_rows, w_qkv, preferred_element_type=jnp.flo...  10.6 us
    reduce_sum x1, other arithmetic, attend_pair(): total = jnp.sum(weights, -1, keepdims=True)  8.42 us
  transfers between devices with their start and end apart: 3, of which 3 were waited for; matrix products, arithmetic and copies ran while one was open for 2% of the time, Pallas kernels for 0%

commit v1 on v0

--- a/solution.py
+++ b/solution.py
@@ -106,7 +106,7 @@
     summed = lax.psum_scatter(
         part.astype(jnp.bfloat16), "tp", scatter_dimension=1, tiled=True
     ).astype(jnp.float32)
-    square = lax.psum(jnp.sum(summed * summed, -1), "tp")
+    square = lax.all_gather(jnp.sum(summed * summed, -1), "tp").sum(axis=0)
     out = (
         local_rows.astype(jnp.float32)
         + summed * lax.rsqrt(square[:, None] / full_width + norm_eps) * post_gain

time: 335 us -> 353 us (1.054)
  blocking collectives: 53.6 us -> 68.2 us
    unnamed x0 -> x1, blocking collectives: none -> 32.6 us
    psum x1 -> x0, blocking collectives: 18 us -> none  [body(): square = lax.psum(jnp.sum(summed * summed, -1), 'tp')]
where the time goes in v1:
time: 353 us; the launch traced here: 352 us
  waiting for transfers between devices  197 us (56%)
  blocking collectives  68.2 us (19%)
  other arithmetic  28.7 us (8%)
  matrix products  26.4 us (7%)
  between operations  17.1 us (5%)
  starting transfers between devices  7.67 us (2%)
  local copies, waits for them, and re-layouts  7.46 us (2%)
    all_gather x1, waiting for transfers between devices, body(): all_rows = lax.all_gather(local_rows, 'tp', axis=1, tiled=True)  92.7 us
    reduce_scatter x1, waiting for transfers between devices, body(): lax.psum_scatter(part.astype(jnp.bfloat16), 'tp', scatter_dimension=1, ti...  87.3 us
    unnamed x1, blocking collectives  32.6 us
    psum x1, blocking collectives, body(): lax.psum((jnp.sum(query_raw * query_raw, -1), jnp.sum(key_raw * key_raw,...  18.3 us
    all_to_all x1, blocking collectives, body(): ret = lax.all_to_all(back, 'seq', 0, 0, tiled=True)  17.3 us
    all_to_all x1, waiting for transfers between devices, body(): got = lax.all_to_all(qkv, 'seq', 0, 0, tiled=True)  16.7 us
    dot_general x1, matrix products, body(): jnp.einsum('tn,cnf->ctf', all_rows, w_qkv, preferred_element_type=jnp.flo...  12.3 us
    reduce_sum x1, other arithmetic, attend_pair(): total = jnp.sum(weights, -1, keepdims=True)  8.42 us
  transfers between devices with their start and end apart: 3, of which 3 were waited for; matrix products, arithmetic and copies ran while one was open for 2% of the time, Pallas kernels for 0%

profile of v1, /device:TPU:4, one launch (start us, length us, event | category | flops | bytes accessed | tf_op | source)
XLA Modules:
  0.0 352.4 jit_solution(13190300521382007325)
XLA Ops:
  7.2 0.0 all-gather.3.cloned.1.call-start
  7.2 1.9 pad_maximum_fusion.2
  9.1 0.0 all-gather.3.cloned.1.call-update
  9.2 1.7 multiply_cosine_fusion
  10.9 92.7 %all-gather.3.cloned.1.call-done = bf16[516,4096]{1,0:T(8,128)(2,1)} async-done(((bf16[516,512]{1,0:T(8,128)(2,1)}), bf16[516,4096]{1,0:T(8,128)(2,1)}) %all-gather.3.cloned.1.call-update) | async-done | bytes 4227088 | tf_op jit(solution)/shard_map/all_gather | solution.py:62
  103.7 12.3 %fusion.45 = (bf16[3,516,512]{2,1,0:T(8,128)(2,1)S(1)}, f32[3,516,512]{2,1,0:T(8,128)}) fusion(bf16[3,4096,512]{2,1,0:T(8,128)(2,1)} %param.10, bf16[516,4096]{1,0:T(8,128)(2,1)} %all-gather.3.cloned.1.call-done), kind=kOutput, calls=%fused_computation.82 | convolution fusion | flops 6493575168 | bytes 21565440 | tf_op jit(solution)/shard_map/tn,cnf->ctf/dot_general | solution.py:63
  116.0 0.1 stack.14
  116.2 1.1 copy.17
  117.3 0.1 copy-done.4
  117.3 1.9 multiply_reduce_fusion.1
  119.2 0.4 squeeze.27
  119.6 0.0 copy-start.6
  119.6 0.4 squeeze.28
  120.0 0.0 copy-start.7
  120.0 18.3 %all-reduce.1 = (f32[516]{0:T(1024)S(1)}, f32[516]{0:T(1024)S(1)}) all-reduce(f32[516]{0:T(1024)S(1)} %get-tuple-element.3, f32[516]{0:T(1024)S(1)} %get-tuple-element.2), channel_id=1, replica_groups=mesh['seq'=16,'tp'=8] {'tp'}, use_global_device_ids=true, to_apply=%region_3.0 | all-reduce | flops 1032 | bytes 8256 | tf_op jit(solution)/shard_map/psum | solution.py:65
  138.4 1.5 multiply_multiply_fusion.1
  139.9 1.5 multiply_multiply_fusion
  141.5 1.7 add_convert_fusion.1
  143.2 0.7 fusion.26
  143.9 0.1 copy.16
  144.0 0.0 copy-start.2
  144.1 0.7 fusion.27
  144.8 0.0 copy-done
  144.8 0.1 copy.15
  144.9 0.2 copy-done.2
  145.1 1.3 pad_maximum_fusion
  146.4 7.4 %all-to-all-start = ((bf16[16,3,128,128]{3,2,1,0:T(8,128)(2,1)}), bf16[16,3,128,128]{3,2,1,0:T(8,128)(2,1)S(1)}, u32[]{:S(2)}, u32[]{:S(2)}) async-start(bf16[16,3,128,128]{3,2,1,0:T(8,128)(2,1)} %bitcast.10), calls=%async_computation | async-start | bytes 3145728 | tf_op jit(solution)/shard_map/all_to_all | solution.py:86
  153.8 0.2 reduce-scatter.2.cloned.1.call-start
  154.1 0.6 dynamic_slice.12
  154.6 0.7 iota_compare_fusion.1
  155.3 0.7 slice.101
  156.0 0.8 pad_maximum_fusion.4
  156.8 0.1 pad_maximum_fusion.3
  156.9 0.6 fusion.34
  158.1 16.7 %all-to-all-done = bf16[16,3,128,128]{3,2,1,0:T(8,128)(2,1)S(1)} async-done(((bf16[16,3,128,128]{3,2,1,0:T(8,128)(2,1)}), bf16[16,3,128,128]{3,2,1,0:T(8,128)(2,1)S(1)}, u32[]{:S(2)}, u32[]{:S(2)}) %all-to-all-start) | async-done | bytes 1572896 | tf_op jit(solution)/shard_map/all_to_all | solution.py:86
  174.8 0.1 fusion.44
  174.9 0.2 fusion.38
  175.1 1.3 fusion.28
  177.0 1.3 fusion.29
  179.0 5.9 %fusion.1 = (f32[2048]{0:T(1024)S(1)}, f32[2048,2048]{0,1:T(8,128)S(1)}) fusion(pred[2048]{0:T(1024)(128)(4,1)S(1)} %iota_compare_fusion.1, bf16[2048,128]{1,0:T(8,128)(2,1)S(1)} %bitcast.93, bf16[2048,128]{1,0:T(8,128)(2,1)S(1)} %bitcast.89), kind=kOutput, calls=%fused_computation.4 | convolution fusion | flops 1094711296 | bytes 17836032 | tf_op jit(solution)/shard_map/dot_general | solution.py:26
  184.9 8.4 %fusion.6 = f32[2048]{0:T(1024)S(1)} fusion(f32[2048]{0:T(1024)S(1)} %get-tuple-element.23, f32[2048,2048]{0,1:T(8,128)S(1)} %get-tuple-element.24, pred[2048]{0:T(1024)(128)(4,1)S(1)} %iota_compare_fusion.1), kind=kLoop, calls=%fused_computation.10 | loop fusion | flops 29358080 | bytes 16795648 | tf_op jit(solution)/shard_map/reduce_sum | solution.py:33
  193.3 3.5 fusion.10
  196.8 0.2 fusion.18
  197.1 0.0 copy-start.10
  197.1 17.3 %all_to_all.10 = bf16[16,136,128]{2,1,0:T(8,128)(2,1)S(1)} all-to-all(bf16[16,136,128]{2,1,0:T(8,128)(2,1)S(1)} %pad_maximum_fusion.1), channel_id=1, replica_groups=mesh['seq'=16,'tp'=8] {'seq'}, dimensions={0} | all-to-all | bytes 1114112 | tf_op jit(solution)/shard_map/all_to_all | solution.py:100
  214.4 0.1 copy.18
  214.5 0.2 slice_bitcast_fusion
  214.7 0.2 copy.19
  214.8 0.1 copy.27
  214.9 4.4 %convolution_convert_fusion = bf16[516,4096]{1,0:T(8,128)(2,1)} fusion(bf16[512,4096]{1,0:T(8,128)(2,1)S(1)} %copy-done.10, bf16[4,512]{1,0:T(4,128)(2,1)S(1)} %bitcast.99, bf16[512,512]{1,0:T(8,128)(2,1)S(1)} %bitcast.92), kind=kOutput, calls=%fused_computation.7 | convolution fusion | flops 2167431168 | bytes 8949760 | tf_op jit(solution)/shard_map/dot_general | solution.py:105
  219.3 0.0 reduce-scatter.2.cloned.1.call-update
  219.3 0.6 copy-done.11
  220.0 0.6 dynamic-slice
  221.2 87.3 %reduce-scatter.2.cloned.1.call-done = bf16[516,512]{1,0:T(8,128)(2,1)} async-done(((bf16[516,4096]{1,0:T(8,128)(2,1)}), bf16[516,512]{1,0:T(8,128)(2,1)}) %reduce-scatter.2.cloned.1.call-update) | async-done | bytes 528400 | tf_op jit(solution)/shard_map/reduce_scatter | solution.py:106
  308.5 1.2 fusion.19
  309.7 0.3 dynamic-update-slice
  310.0 32.6 %all-reduce = f32[4128]{0:T(1024)S(1)} all-reduce(f32[4128]{0:T(1024)S(1)} %dynamic-update-slice), channel_id=2, replica_groups=mesh['seq'=16,'tp'=8] {'tp'}, use_global_device_ids=true, to_apply=%add | all-reduce | flops 4128 | bytes 33024
  342.6 0.1 reshape.209
  342.8 0.0 copy-done.1
  342.8 0.0 copy-done.5
  342.8 0.0 copy-done.8
  342.8 1.3 fusion.22
  344.1 0.8 slice.104
  344.9 0.6 slice.105
  (28 shorter events, 0.2 us)
Async XLA Ops:
  7.2 2.0 copy-start.9
  7.2 96.5 %all-gather.3.cloned.1.call-start = ((), (), s32[]{:S(2)}) async-start(), calls=%async_computation.3 | async-start | bytes 4792320 | tf_op jit(solution)/shard_map/all_gather | solution.py:62
  116.0 1.4 copy-start.4
  119.6 18.7 %copy-start.6 = (f32[512]{0:T(512)S(1)}, f32[512]{0:T(512)}, u32[]{:S(2)}) copy-start(f32[512]{0:T(512)} %param.12) | copy-start | bytes 6148
  120.0 19.9 %copy-start.7 = (f32[512]{0:T(512)S(1)}, f32[512]{0:T(512)}, u32[]{:S(2)}) copy-start(f32[512]{0:T(512)} %param.13) | copy-start | bytes 6148
  139.9 1.6 copy-start.3
  143.2 1.6 copy-start
  144.0 1.0 copy-start.2
  146.4 28.4 %all-to-all-start = ((bf16[16,3,128,128]{3,2,1,0:T(8,128)(2,1)}), bf16[16,3,128,128]{3,2,1,0:T(8,128)(2,1)S(1)}, u32[]{:S(2)}, u32[]{:S(2)}) async-start(bf16[16,3,128,128]{3,2,1,0:T(8,128)(2,1)} %bitcast.10), calls=%async_computation | async-start | bytes 3145728 | tf_op jit(solution)/shard_map/all_to_all | solution.py:86
  153.8 154.7 %reduce-scatter.2.cloned.1.call-start = ((), (), s32[]{:S(2)}) async-start(), calls=%async_computation.4 | async-start | bytes 4792320 | tf_op jit(solution)/shard_map/reduce_scatter | solution.py:106
  197.1 17.9 %copy-start.10 = (bf16[512,4096]{1,0:T(8,128)(2,1)S(1)}, bf16[512,4096]{1,0:T(8,128)(2,1)}, u32[]{:S(2)}) copy-start(bf16[512,4096]{1,0:T(8,128)(2,1)} %param.11) | copy-start | bytes 12582916
  219.3 0.7 copy-start.11
  219.3 123.5 %copy-start.1 = (bf16[4,128,512]{2,1,0:T(8,128)(2,1)S(1)}, bf16[4,128,512]{2,1,0:T(8,128)(2,1)}, u32[]{:S(2)}) copy-start(bf16[4,128,512]{2,1,0:T(8,128)(2,1)} %param.8) | copy-start | bytes 1572868
  219.3 123.5 %copy-start.5 = (bf16[4,512]{1,0:T(4,128)(2,1)S(1)}, bf16[4,512]{1,0:T(4,128)(2,1)}, u32[]{:S(2)}) copy-start(bf16[4,512]{1,0:T(4,128)(2,1)} %param.9) | copy-start | bytes 12292
  219.3 123.5 %copy-start.8 = (f32[512]{0:T(512)S(1)}, f32[512]{0:T(512)}, u32[]{:S(2)}) copy-start(f32[512]{0:T(512)} %param.14) | copy-start | bytes 6148
Sparse Core Ops, SparseCore 0:
  9.7 93.9 all-gather.2
  219.5 88.9 reduce-scatter.1
